TPU v7x, 256 devices: a whole 4x4x8 slice. The times are simulated.
256 devices in a mesh: win: 32 (over x, y, core), exp: 8 (over z).
Axes of the slice: x: 4, y: 4, z: 8, core: 2. Of those that a mesh axis runs over, the one named last changes fastest.
Arguments:
- tokens: bfloat16 [16384, 2048], P('win'), may hold values from -9 to 9
- router: bfloat16 [2048, 32], replicated, may hold values from -0.125 to 0.125
- w_in: bfloat16 [32, 2048, 8192], P('win', None, 'exp'), may hold values from -0.125 to 0.125
- w_out: bfloat16 [32, 8192, 2048], P('win', 'exp'), may hold values from -0.0625 to 0.0625
- expert_ids: int32 [16384, 2], P('win'), may hold values from 0 to 31, all different within a row; in each aligned block of 512 rows (0 to 511, 512 to 1023, ...) at most 48 rows name the same one
- offsets: int32 [32], P('win'), may hold values from 0 to 63
Outputs:
- consensus_state: bfloat16 [16384, 2048], P('win', 'exp')
Inputs may be any that keep to these rules, and one draw needn't show every extreme that they name: `expert_ids`: in each window (an aligned block of 512 rows) no expert is named by more than 48 choices, a bound that some block reaches; a token's two experts differ.
All inputs are finite; a program needn't handle non-finite values.
Results may differ from a plain program's by a relative error of at most 0.015.
Values may be sent and summed in bfloat16 or wider, within the bound.
No kernel may reach another device: no remote copies, remote signals or barrier semaphores. Data moves between devices by JAX's collectives and lax.ppermute only.
A program may use at most 128 MiB of HBM per device.

v0:
```python
import math
import jax
import jax.numpy as jnp
from jax import lax
from jax.sharding import PartitionSpec as P

D = 2048
EXPERTS = 32
OV = 256
CAP = 48


def shifted(shard, axis, by):
    count = lax.axis_size(axis)
    pairs = [(i, i + by) for i in range(count) if 0 <= i + by < count]
    return lax.ppermute(shard, axis, pairs)


def shards(tokens, router, w_in, w_out, expert_ids, offsets):
    tok_count = tokens.shape[0]
    win_size = lax.axis_size("win")
    local_experts = w_in.shape[0]
    col_width = D // lax.axis_size("exp")
    flat_ids = expert_ids.reshape(-1)
    expert_order = jnp.arange(EXPERTS, dtype=jnp.int32)
    hit_table = (flat_ids[:, None] == expert_order[None, :]).astype(jnp.int32)
    rank_table = jnp.cumsum(hit_table, axis=0) - 1
    slot_index = jnp.sum(hit_table * rank_table, axis=1)
    slot_target = flat_ids * CAP + slot_index
    token_index = jnp.repeat(jnp.arange(tok_count, dtype=jnp.int32), 2)
    source_table = jnp.full((EXPERTS * CAP,), tok_count, jnp.int32).at[slot_target].set(token_index)
    padded = jnp.concatenate([tokens, jnp.zeros((1, D), tokens.dtype)], axis=0)
    outgoing = padded[source_table].reshape(win_size, local_experts, CAP, D)
    hidden_rows = jnp.einsum(
        "secd,edf->secf",
        lax.all_to_all(outgoing, "win", split_axis=0, concat_axis=0, tiled=True),
        w_in,
        preferred_element_type=jnp.float32,
    )
    hidden_rows = jax.nn.relu(hidden_rows).astype(jnp.bfloat16)
    results = jnp.einsum("secf,efd->secd", hidden_rows, w_out, preferred_element_type=jnp.float32)
    logits = jnp.dot(tokens, router, preferred_element_type=jnp.float32)
    first_hit = expert_ids[:, 0:1] == expert_order[None, :]
    second_hit = expert_ids[:, 1:2] == expert_order[None, :]
    logit_first = jnp.sum(jnp.where(first_hit, logits, 0.0), axis=1, keepdims=True)
    logit_second = jnp.sum(jnp.where(second_hit, logits, 0.0), axis=1, keepdims=True)
    gate_first = jax.nn.sigmoid(logit_first - logit_second)
    gate_second = jax.nn.sigmoid(logit_second - logit_first)
    returned = lax.all_to_all(results, "win", split_axis=0, concat_axis=0, tiled=True)
    flat_rows = returned.reshape(EXPERTS * CAP, returned.shape[-1])
    picked = flat_rows[slot_target].reshape(tok_count, 2, returned.shape[-1])
    expert_sum = lax.psum_scatter(
        gate_first * picked[:, 0] + gate_second * picked[:, 1],
        "exp",
        scatter_dimension=1,
        tiled=True,
    )
    own_cols = lax.dynamic_slice_in_dim(tokens, lax.axis_index("exp") * col_width, col_width, 1)
    layer_state = (own_cols.astype(jnp.float32) + expert_sum).astype(jnp.bfloat16)
    head_rows = layer_state[:OV]
    tail_rows = layer_state[tok_count - OV :]
    previous = shifted(tail_rows, "win", 1)
    contract = (((1,), (1,)), ((), ()))
    partial_scores = lax.dot_general(
        head_rows, previous, contract, preferred_element_type=jnp.float32
    )
    scores = lax.psum(partial_scores.astype(jnp.bfloat16), "exp").astype(jnp.float32)
    row_pos = jnp.arange(OV, dtype=jnp.int32)[:, None]
    col_pos = jnp.arange(OV, dtype=jnp.int32)[None, :]
    distance = jnp.abs(col_pos - row_pos - offsets[0]).astype(jnp.float32) * (8.0 / OV)
    scores = scores / math.sqrt(D) - distance
    weights = jax.nn.softmax(scores, axis=-1).astype(jnp.bfloat16)
    blended = jnp.dot(weights, previous, preferred_element_type=jnp.float32)
    mixed_rows = (0.5 * (head_rows.astype(jnp.float32) + blended)).astype(jnp.bfloat16)
    mixed_rows = jnp.where(lax.axis_index("win") > 0, mixed_rows, head_rows)
    return jnp.concatenate([mixed_rows, layer_state[OV:]], axis=0)


def solution(mesh):
    return jax.shard_map(
        shards,
        mesh=mesh,
        in_specs=(
            P("win", None),
            P(),
            P("win", None, "exp"),
            P("win", "exp", None),
            P("win", None),
            P("win"),
        ),
        out_specs=P("win", "exp"),
        check_vma=False,
    )
```

profile of v0, /device:TPU:2, one launch (start us, length us, event | category | flops | bytes accessed | tf_op | source)
XLA Modules:
  0.0 520.1 jit_solution(12146455405890550260)
XLA Ops:
  6.5 0.0 copy-start
  6.5 0.9 copy.15
  7.4 0.2 eq.67
  7.6 0.2 eq.63
  7.7 0.7 broadcast_multiply_fusion
  8.4 9.0 %reduce-window.6 = s32[32,8,128]{2,1,0:T(8,128)S(1)} reduce-window(s32[32,8,128]{2,1,0:T(8,128)S(1)} %fusion.20, s32[]{:T(128)} %constant.20.clone.1), window={size=1x1x128 pad=0_0x0_0x127_0}, to_apply=%region_2.3 | reduce-window | flops 4161536 | bytes 262148 | tf_op jit(solution)/shard_map/reduce-window
  17.5 0.1 slice.37
  17.6 0.1 copy.17
  17.7 0.1 copy.18
  17.8 0.1 add_add_fusion
  17.9 0.1 copy.14
  18.1 0.2 mul.54
  18.3 0.2 reshape.133
  18.5 4.3 scatter_custom_fusion
  22.9 1.7 concatenate.6
  24.6 7.1 %gather_fusion = bf16[1536,2048]{1,0:T(8,128)(2,1)} fusion(bf16[513,2048]{1,0:T(8,128)(2,1)S(1)} %concatenate.6, s32[2048]{0:T(1024)S(1)} %pad_clamp_fusion), kind=kCustom, calls=%fused_computation | custom fusion | bytes 12589056 | tf_op jit(solution)/shard_map/gather | solution.py:33
  31.7 0.0 copy-start.3
  31.7 78.5 %all_to_all.10 = bf16[32,1,48,2048]{3,2,1,0:T(8,128)(2,1)S(1)} all-to-all(bf16[32,1,48,2048]{3,2,1,0:T(8,128)(2,1)} %bitcast.61), channel_id=1, replica_groups=mesh['win'=32,'exp'=8] {'win'}, dimensions={0} | all-to-all | bytes 12582912 | tf_op jit(solution)/shard_map/all_to_all | solution.py:36
  110.2 0.0 copy-done.3
  110.2 0.0 copy-start.4
  110.2 6.8 %fusion = bf16[32,48,1024]{2,1,0:T(8,128)(2,1)S(1)} fusion(bf16[32,1,48,2048]{3,2,1,0:T(8,128)(2,1)S(1)} %all_to_all.10, bf16[1,2048,1024]{2,1,0:T(8,128)(2,1)S(1)} %copy-done.3), kind=kOutput, calls=%fused_computation.3 | convolution fusion | flops 6442450944 | bytes 13631488 | tf_op jit(solution)/shard_map/secd,edf->secf/dot_general | solution.py:34
  117.0 0.0 copy-done.4
  117.0 9.1 %convolution_bitcast_fusion = f32[32,1,48,2048]{3,2,1,0:T(8,128)} fusion(bf16[1,1024,2048]{2,1,0:T(8,128)(2,1)S(1)} %copy-done.4, bf16[32,48,1024]{2,1,0:T(8,128)(2,1)S(1)} %fusion), kind=kOutput, calls=%fused_computation.6 | convolution fusion | flops 6447169536 | bytes 19922944 | tf_op jit(solution)/shard_map/secf,efd->secd/dot_general | solution.py:41
  126.1 0.0 copy-start.2
  126.1 0.0 copy-start.1
  126.1 7.4 %all-to-all-start.1 = ((f32[32,1,48,2048]{3,2,1,0:T(8,128)}), f32[32,1,48,2048]{3,2,1,0:T(8,128)}, u32[]{:S(2)}, u32[]{:S(2)}) async-start(f32[32,1,48,2048]{3,2,1,0:T(8,128)} %convolution_bitcast_fusion), calls=%async_computation.1 | async-start | bytes 25165824 | tf_op jit(solution)/shard_map/all_to_all | solution.py:49
  133.5 0.2 reduce-scatter.2.cloned.1.call-start
  133.8 0.0 copy-done.2
  133.8 0.0 copy-done
  133.8 0.0 copy-done.1
  133.8 0.8 select_reduce_fusion.1
  134.6 165.8 %all-to-all-done.1 = f32[32,1,48,2048]{3,2,1,0:T(8,128)} async-done(((f32[32,1,48,2048]{3,2,1,0:T(8,128)}), f32[32,1,48,2048]{3,2,1,0:T(8,128)}, u32[]{:S(2)}, u32[]{:S(2)}) %all-to-all-start.1) | async-done | bytes 12582944 | tf_op jit(solution)/shard_map/all_to_all | solution.py:49
  300.4 13.6 %gather_fusion.1 = f32[1024,2048]{1,0:T(8,128)} fusion(f32[1536,2048]{1,0:T(8,128)} %bitcast.17, s32[1024]{0:T(1024)S(1)} %broadcast_clamp_fusion), kind=kCustom, calls=%fused_computation.1 | custom fusion | bytes 16781312 | tf_op jit(solution)/shard_map/gather | solution.py:51
  314.1 10.6 %reshape.112 = f32[512,2,2048]{2,1,0:T(2,128)} reshape(f32[1024,2048]{1,0:T(8,128)} %gather_fusion.1) | data formatting | bytes 16777216 | tf_op jit(solution)/shard_map/reshape | solution.py:51
  324.6 11.0 %fusion.27 = (f32[512,1,2048]{2,1,0:T(1,128)S(1)}, f32[512,1,2048]{2,1,0:T(1,128)S(1)}) fusion(f32[512,2,2048]{2,1,0:T(2,128)} %reshape.112), kind=kLoop, calls=%fused_computation.56 | loop fusion | bytes 16777216 | tf_op jit(solution)/shard_map/slice | solution.py:53
  335.7 6.7 %fusion.3 = f32[512,2048]{1,0:T(8,128)} fusion(f32[512,1,2048]{2,1,0:T(1,128)S(1)} %get-tuple-element.8, f32[512,1,2048]{2,1,0:T(1,128)S(1)} %get-tuple-element.7, f32[512]{0:T(512)S(1)} %get-tuple-element.10, f32[512]{0:T(512)S(1)} %get-tuple-element.9), kind=kLoop, calls=%fused_computation.9 | loop fusion | flops 3145728 | bytes 12587008 | tf_op jit(solution)/shard_map/add | solution.py:53
  342.4 0.0 reduce-scatter.2.cloned.1.call-update
  342.4 0.0 all-reduce.3.cloned.1.call-start
  342.5 87.0 %reduce-scatter.2.cloned.1.call-done = f32[512,256]{1,0:T(8,128)} async-done(((f32[512,2048]{1,0:T(8,128)}), f32[512,256]{1,0:T(8,128)}) %reduce-scatter.2.cloned.1.call-update) | async-done | bytes 524304 | tf_op jit(solution)/shard_map/reduce_scatter | solution.py:52
  429.5 1.1 add_convert_fusion
  430.7 1.9 collective-permute-start
  432.6 6.5 %collective-permute-done = bf16[256,256]{1,0:T(8,128)(2,1)S(1)} collective-permute-done((bf16[256,256]{1,0:T(8,128)(2,1)S(1)}, bf16[256,256]{1,0:T(8,128)(2,1)S(1)}, u32[]{:S(2)}, u32[]{:S(2)}) %collective-permute-start) | collective-permute-done | bytes 131104 | tf_op jit(solution)/shard_map/ppermute | solution.py:16
  439.1 0.9 convolution_convert_fusion
  439.9 0.0 all-reduce.3.cloned.1.call-update
  440.6 68.6 %all-reduce.3.cloned.1.call-done = bf16[256,256]{1,0:T(8,128)(2,1)} async-done(((bf16[256,256]{1,0:T(8,128)(2,1)}), bf16[256,256]{1,0:T(8,128)(2,1)}) %all-reduce.3.cloned.1.call-update) | async-done | bytes 131088 | tf_op jit(solution)/shard_map/psum | solution.py:67
  509.2 1.1 fusion.11
  510.3 1.1 fusion.12
  511.4 1.2 fusion.10
  512.6 0.7 pad_maximum_fusion
  (12 shorter events, 0.2 us)
Async XLA Ops:
  6.5 127.3 %copy-start = (bf16[2048,32]{0,1:T(8,128)(2,1)S(1)}, bf16[2048,32]{0,1:T(8,128)(2,1)}, u32[]{:S(2)}) copy-start(bf16[2048,32]{0,1:T(8,128)(2,1)} %param.7) | copy-start | bytes 393220
  31.7 78.5 %copy-start.3 = (bf16[1,2048,1024]{2,1,0:T(8,128)(2,1)S(1)}, bf16[1,2048,1024]{2,1,0:T(8,128)(2,1)}, u32[]{:S(2)}) copy-start(bf16[1,2048,1024]{2,1,0:T(8,128)(2,1)} %param.8) | copy-start | bytes 12582916
  110.2 6.8 %copy-start.4 = (bf16[1,1024,2048]{2,1,0:T(8,128)(2,1)S(1)}, bf16[1,1024,2048]{2,1,0:T(8,128)(2,1)}, u32[]{:S(2)}) copy-start(bf16[1,1024,2048]{2,1,0:T(8,128)(2,1)} %param.9) | copy-start | bytes 12582916
  126.1 7.7 %copy-start.2 = (s32[512,2]{0,1:T(2,128)S(1)}, s32[512,2]{0,1:T(2,128)}, u32[]{:S(2)}) copy-start(s32[512,2]{0,1:T(2,128)} %param.10) | copy-start | bytes 12292
  126.1 7.7 %copy-start.1 = (bf16[512,2048]{1,0:T(8,128)(2,1)S(1)}, bf16[512,2048]{1,0:T(8,128)(2,1)}, u32[]{:S(2)}) copy-start(bf16[512,2048]{1,0:T(8,128)(2,1)} %param.6) | copy-start | bytes 6291460
  126.1 174.3 %all-to-all-start.1 = ((f32[32,1,48,2048]{3,2,1,0:T(8,128)}), f32[32,1,48,2048]{3,2,1,0:T(8,128)}, u32[]{:S(2)}, u32[]{:S(2)}) async-start(f32[32,1,48,2048]{3,2,1,0:T(8,128)} %convolution_bitcast_fusion), calls=%async_computation.1 | async-start | bytes 25165824 | tf_op jit(solution)/shard_map/all_to_all | solution.py:49
  133.5 296.0 %reduce-scatter.2.cloned.1.call-start = ((), (), s32[]{:S(2)}) async-start(), calls=%async_computation.3 | async-start | bytes 4718592 | tf_op jit(solution)/shard_map/reduce_scatter | solution.py:52
  342.4 166.8 %all-reduce.3.cloned.1.call-start = ((), (), s32[]{:S(2)}) async-start(), calls=%async_computation.4 | async-start | bytes 262144 | tf_op jit(solution)/shard_map/psum | solution.py:67
  430.7 8.4 %collective-permute-start = (bf16[256,256]{1,0:T(8,128)(2,1)S(1)}, bf16[256,256]{1,0:T(8,128)(2,1)S(1)}, u32[]{:S(2)}, u32[]{:S(2)}) collective-permute-start(bf16[256,256]{1,0:T(8,128)(2,1)S(1)} %slice.42), channel_id=1, source_target_pairs={{0,8},{8,16},{16,24},{24,32},{32,40},{40,48},{48,56},{56,64},{64,7... | collective-permute-start | bytes 393224 | tf_op jit(solution)/shard_map/ppermute | solution.py:16
Sparse Core Ops, SparseCore 0:
  342.5 86.9 reduce-scatter.1
  440.1 69.0 all-reduce.2
where the time goes:
time: 521 us; the launch traced here: 520 us
  waiting for transfers between devices  328 us (63%)
  blocking collectives  78.5 us (15%)
  local copies, waits for them, and re-layouts  50.4 us (10%)
  other arithmetic  20.7 us (4%)
  matrix products  18.7 us (4%)
  between operations  14.3 us (3%)
  starting transfers between devices  9.6 us (2%)
    all_to_all x1, waiting for transfers between devices, shards(): lax.all_to_all(results, 'win', split_axis=0, concat_axis=0, tiled=True)  166 us
    reduce_scatter x1, waiting for transfers between devices, shards(): lax.psum_scatter(gate_first * picked[:, 0] + gate_second * picked[:, 1],...  87 us
    all_to_all x1, blocking collectives, shards(): lax.all_to_all(outgoing, 'win', split_axis=0, concat_axis=0, tiled=True)  78.5 us
    psum x1, waiting for transfers between devices, shards(): lax.psum(partial_scores.astype(jnp.bfloat16), 'exp').astype(jnp.float32)  68.6 us
    gather x1, local copies, waits for them, and re-layouts, shards(): picked = flat_rows[slot_target].reshape(tok_count, 2, returned.shape[-1])  13.6 us
    slice x1, local copies, waits for them, and re-layouts, shards(): picked[:, 0]  11 us
    reshape x1, local copies, waits for them, and re-layouts, shards(): picked = flat_rows[slot_target].reshape(tok_count, 2, returned.shape[-1])  10.6 us
  transfers between devices with their start and end apart: 4, of which 4 were waited for; matrix products, arithmetic and copies ran while one was open for 0% of the time, Pallas kernels for 0%

commit v1 on v0

--- a/solution.py
+++ b/solution.py
@@ -64,7 +64,9 @@
     partial_scores = lax.dot_general(
         head_rows, previous, contract, preferred_element_type=jnp.float32
     )
-    scores = lax.psum(partial_scores.astype(jnp.bfloat16), "exp").astype(jnp.float32)
+    scores = jnp.sum(lax.all_gather(partial_scores.astype(jnp.bfloat16), "exp"), axis=0).astype(
+        jnp.float32
+    )
     row_pos = jnp.arange(OV, dtype=jnp.int32)[:, None]
     col_pos = jnp.arange(OV, dtype=jnp.int32)[None, :]
     distance = jnp.abs(col_pos - row_pos - offsets[0]).astype(jnp.float32) * (8.0 / OV)

time: 521 us -> 485 us (0.931)
  waiting for transfers between devices: 328 us -> 294 us
    psum x1 -> x0, waiting for transfers between devices: 68.6 us -> none  [shards(): lax.psum(partial_scores.astype(jnp.bfloat16), 'exp').astype(jnp.float32)]
    all_gather x0 -> x1, waiting for transfers between devices: none -> 34.4 us  [shards(): lax.all_gather(partial_scores.astype(jnp.bfloat16), 'exp')]
where the time goes in v1:
time: 485 us
  waiting for transfers between devices  294 us (61%)
  blocking collectives  78.5 us (16%)
  local copies, waits for them, and re-layouts  50.4 us (10%)
  other arithmetic  20.3 us (4%)
  matrix products  17.8 us (4%)
  between operations  14.3 us (3%)
  starting transfers between devices  9.6 us (2%)
    all_to_all x1, waiting for transfers between devices, shards(): lax.all_to_all(results, 'win', split_axis=0, concat_axis=0, tiled=True)  166 us
    reduce_scatter x1, waiting for transfers between devices, shards(): lax.psum_scatter(gate_first * picked[:, 0] + gate_second * picked[:, 1],...  87 us
    all_to_all x1, blocking collectives, shards(): lax.all_to_all(outgoing, 'win', split_axis=0, concat_axis=0, tiled=True)  78.5 us
    all_gather x1, waiting for transfers between devices, shards(): lax.all_gather(partial_scores.astype(jnp.bfloat16), 'exp')  34.4 us
    gather x1, local copies, waits for them, and re-layouts, shards(): picked = flat_rows[slot_target].reshape(tok_count, 2, returned.shape[-1])  13.6 us
    slice x1, local copies, waits for them, and re-layouts, shards(): picked[:, 0]  11 us
    reshape x1, local copies, waits for them, and re-layouts, shards(): picked = flat_rows[slot_target].reshape(tok_count, 2, returned.shape[-1])  10.6 us
  transfers between devices with their start and end apart: 4, of which 4 were waited for; matrix products, arithmetic and copies ran while one was open for 0% of the time, Pallas kernels for 0%

profile of v1, /device:TPU:2, one launch (start us, length us, event | category | flops | bytes accessed | tf_op | source)
XLA Modules:
  0.0 484.7 jit_solution(4257872956064617419)
XLA Ops:
  6.5 0.0 copy-start
  6.5 0.9 copy.24
  7.4 0.2 eq.67
  7.6 0.2 eq.63
  7.7 0.7 broadcast_multiply_fusion
  8.4 9.0 %reduce-window.6 = s32[32,8,128]{2,1,0:T(8,128)S(1)} reduce-window(s32[32,8,128]{2,1,0:T(8,128)S(1)} %fusion.20, s32[]{:T(128)} %constant.20.clone.1), window={size=1x1x128 pad=0_0x0_0x127_0}, to_apply=%region_2.3 | reduce-window | flops 4161536 | bytes 262148 | tf_op jit(solution)/shard_map/reduce-window
  17.5 0.1 slice.37
  17.6 0.1 copy.26
  17.7 0.1 copy.27
  17.8 0.1 add_add_fusion
  17.9 0.1 copy.23
  18.1 0.2 mul.54
  18.3 0.2 reshape.133
  18.5 4.3 scatter_custom_fusion
  22.9 1.7 concatenate.6
  24.6 7.1 %gather_fusion = bf16[1536,2048]{1,0:T(8,128)(2,1)} fusion(bf16[513,2048]{1,0:T(8,128)(2,1)S(1)} %concatenate.6, s32[2048]{0:T(1024)S(1)} %pad_clamp_fusion), kind=kCustom, calls=%fused_computation | custom fusion | bytes 12589056 | tf_op jit(solution)/shard_map/gather | solution.py:33
  31.7 0.0 copy-start.3
  31.7 78.5 %all_to_all.10 = bf16[32,1,48,2048]{3,2,1,0:T(8,128)(2,1)S(1)} all-to-all(bf16[32,1,48,2048]{3,2,1,0:T(8,128)(2,1)} %bitcast.62), channel_id=1, replica_groups=mesh['win'=32,'exp'=8] {'win'}, dimensions={0} | all-to-all | bytes 12582912 | tf_op jit(solution)/shard_map/all_to_all | solution.py:36
  110.2 0.0 copy-done.3
  110.2 0.0 copy-start.4
  110.2 6.8 %fusion = bf16[32,48,1024]{2,1,0:T(8,128)(2,1)S(1)} fusion(bf16[32,1,48,2048]{3,2,1,0:T(8,128)(2,1)S(1)} %all_to_all.10, bf16[1,2048,1024]{2,1,0:T(8,128)(2,1)S(1)} %copy-done.3), kind=kOutput, calls=%fused_computation.3 | convolution fusion | flops 6442450944 | bytes 13631488 | tf_op jit(solution)/shard_map/secd,edf->secf/dot_general | solution.py:34
  117.0 0.0 copy-done.4
  117.0 9.1 %convolution_bitcast_fusion = f32[32,1,48,2048]{3,2,1,0:T(8,128)} fusion(bf16[1,1024,2048]{2,1,0:T(8,128)(2,1)S(1)} %copy-done.4, bf16[32,48,1024]{2,1,0:T(8,128)(2,1)S(1)} %fusion), kind=kOutput, calls=%fused_computation.6 | convolution fusion | flops 6447169536 | bytes 19922944 | tf_op jit(solution)/shard_map/secf,efd->secd/dot_general | solution.py:41
  126.1 0.0 copy-start.2
  126.1 0.0 copy-start.1
  126.1 7.4 %all-to-all-start.1 = ((f32[32,1,48,2048]{3,2,1,0:T(8,128)}), f32[32,1,48,2048]{3,2,1,0:T(8,128)}, u32[]{:S(2)}, u32[]{:S(2)}) async-start(f32[32,1,48,2048]{3,2,1,0:T(8,128)} %convolution_bitcast_fusion), calls=%async_computation.1 | async-start | bytes 25165824 | tf_op jit(solution)/shard_map/all_to_all | solution.py:49
  133.5 0.2 reduce-scatter.2.cloned.1.call-start
  133.8 0.0 copy-done.2
  133.8 0.0 copy-done
  133.8 0.0 copy-done.1
  133.8 0.8 select_reduce_fusion.1
  134.6 165.8 %all-to-all-done.1 = f32[32,1,48,2048]{3,2,1,0:T(8,128)} async-done(((f32[32,1,48,2048]{3,2,1,0:T(8,128)}), f32[32,1,48,2048]{3,2,1,0:T(8,128)}, u32[]{:S(2)}, u32[]{:S(2)}) %all-to-all-start.1) | async-done | bytes 12582944 | tf_op jit(solution)/shard_map/all_to_all | solution.py:49
  300.4 13.6 %gather_fusion.1 = f32[1024,2048]{1,0:T(8,128)} fusion(f32[1536,2048]{1,0:T(8,128)} %bitcast.17, s32[1024]{0:T(1024)S(1)} %broadcast_clamp_fusion), kind=kCustom, calls=%fused_computation.1 | custom fusion | bytes 16781312 | tf_op jit(solution)/shard_map/gather | solution.py:51
  314.1 10.6 %reshape.112 = f32[512,2,2048]{2,1,0:T(2,128)} reshape(f32[1024,2048]{1,0:T(8,128)} %gather_fusion.1) | data formatting | bytes 16777216 | tf_op jit(solution)/shard_map/reshape | solution.py:51
  324.6 11.0 %fusion.27 = (f32[512,1,2048]{2,1,0:T(1,128)S(1)}, f32[512,1,2048]{2,1,0:T(1,128)S(1)}) fusion(f32[512,2,2048]{2,1,0:T(2,128)} %reshape.112), kind=kLoop, calls=%fused_computation.56 | loop fusion | bytes 16777216 | tf_op jit(solution)/shard_map/slice | solution.py:53
  335.7 6.7 %fusion.3 = f32[512,2048]{1,0:T(8,128)} fusion(f32[512,1,2048]{2,1,0:T(1,128)S(1)} %get-tuple-element.8, f32[512,1,2048]{2,1,0:T(1,128)S(1)} %get-tuple-element.7, f32[512]{0:T(512)S(1)} %get-tuple-element.10, f32[512]{0:T(512)S(1)} %get-tuple-element.9), kind=kLoop, calls=%fused_computation.9 | loop fusion | flops 3145728 | bytes 12587008 | tf_op jit(solution)/shard_map/add | solution.py:53
  342.4 0.0 reduce-scatter.2.cloned.1.call-update
  342.4 0.0 all-gather.3.cloned.1.call-start
  342.5 87.0 %reduce-scatter.2.cloned.1.call-done = f32[512,256]{1,0:T(8,128)} async-done(((f32[512,2048]{1,0:T(8,128)}), f32[512,256]{1,0:T(8,128)}) %reduce-scatter.2.cloned.1.call-update) | async-done | bytes 524304 | tf_op jit(solution)/shard_map/reduce_scatter | solution.py:52
  429.5 1.1 add_convert_fusion
  430.7 1.9 collective-permute-start
  432.6 6.5 %collective-permute-done = bf16[256,256]{1,0:T(8,128)(2,1)S(1)} collective-permute-done((bf16[256,256]{1,0:T(8,128)(2,1)S(1)}, bf16[256,256]{1,0:T(8,128)(2,1)S(1)}, u32[]{:S(2)}, u32[]{:S(2)}) %collective-permute-start) | collective-permute-done | bytes 131104 | tf_op jit(solution)/shard_map/ppermute | solution.py:16
  439.1 0.9 convolution_convert_fusion
  439.9 0.0 all-gather.3.cloned.1.call-update
  440.6 34.4 %all-gather.3.cloned.1.call-done = bf16[2048,256]{1,0:T(8,128)(2,1)} async-done(((bf16[256,256]{1,0:T(8,128)(2,1)}), bf16[2048,256]{1,0:T(8,128)(2,1)}) %all-gather.3.cloned.1.call-update) | async-done | bytes 1048592 | tf_op jit(solution)/shard_map/all_gather | solution.py:67
  475.1 1.4 reduce_sum.54
  476.4 0.2 fusion.11
  476.6 0.2 fusion.12
  476.8 0.3 fusion.10
  477.1 0.7 pad_maximum_fusion
  (12 shorter events, 0.2 us)
Async XLA Ops:
  6.5 127.3 %copy-start = (bf16[2048,32]{0,1:T(8,128)(2,1)S(1)}, bf16[2048,32]{0,1:T(8,128)(2,1)}, u32[]{:S(2)}) copy-start(bf16[2048,32]{0,1:T(8,128)(2,1)} %param.7) | copy-start | bytes 393220
  31.7 78.5 %copy-start.3 = (bf16[1,2048,1024]{2,1,0:T(8,128)(2,1)S(1)}, bf16[1,2048,1024]{2,1,0:T(8,128)(2,1)}, u32[]{:S(2)}) copy-start(bf16[1,2048,1024]{2,1,0:T(8,128)(2,1)} %param.8) | copy-start | bytes 12582916
  110.2 6.8 %copy-start.4 = (bf16[1,1024,2048]{2,1,0:T(8,128)(2,1)S(1)}, bf16[1,1024,2048]{2,1,0:T(8,128)(2,1)}, u32[]{:S(2)}) copy-start(bf16[1,1024,2048]{2,1,0:T(8,128)(2,1)} %param.9) | copy-start | bytes 12582916
  126.1 7.7 %copy-start.2 = (s32[512,2]{0,1:T(2,128)S(1)}, s32[512,2]{0,1:T(2,128)}, u32[]{:S(2)}) copy-start(s32[512,2]{0,1:T(2,128)} %param.10) | copy-start | bytes 12292
  126.1 7.7 %copy-start.1 = (bf16[512,2048]{1,0:T(8,128)(2,1)S(1)}, bf16[512,2048]{1,0:T(8,128)(2,1)}, u32[]{:S(2)}) copy-start(bf16[512,2048]{1,0:T(8,128)(2,1)} %param.6) | copy-start | bytes 6291460
  126.1 174.3 %all-to-all-start.1 = ((f32[32,1,48,2048]{3,2,1,0:T(8,128)}), f32[32,1,48,2048]{3,2,1,0:T(8,128)}, u32[]{:S(2)}, u32[]{:S(2)}) async-start(f32[32,1,48,2048]{3,2,1,0:T(8,128)} %convolution_bitcast_fusion), calls=%async_computation.1 | async-start | bytes 25165824 | tf_op jit(solution)/shard_map/all_to_all | solution.py:49
  133.5 296.0 %reduce-scatter.2.cloned.1.call-start = ((), (), s32[]{:S(2)}) async-start(), calls=%async_computation.3 | async-start | bytes 4718592 | tf_op jit(solution)/shard_map/reduce_scatter | solution.py:52
  342.4 132.6 %all-gather.3.cloned.1.call-start = ((), (), s32[]{:S(2)}) async-start(), calls=%async_computation.4 | async-start | bytes 1179648 | tf_op jit(solution)/shard_map/all_gather | solution.py:67
  430.7 8.4 %collective-permute-start = (bf16[256,256]{1,0:T(8,128)(2,1)S(1)}, bf16[256,256]{1,0:T(8,128)(2,1)S(1)}, u32[]{:S(2)}, u32[]{:S(2)}) collective-permute-start(bf16[256,256]{1,0:T(8,128)(2,1)S(1)} %slice.42), channel_id=1, source_target_pairs={{0,8},{8,16},{16,24},{24,32},{32,40},{40,48},{48,56},{56,64},{64,7... | collective-permute-start | bytes 393224 | tf_op jit(solution)/shard_map/ppermute | solution.py:16
Sparse Core Ops, SparseCore 0:
  342.5 86.9 reduce-scatter.1
  440.1 34.9 all-gather.2
